TPU v7x, 32 devices: a whole 2x2x4 slice. The times are simulated.
32 devices in a mesh: grp: 4 (over x, core), ep: 8 (over z, y).
Axes of the slice: x: 2, y: 2, z: 4, core: 2. Of those that a mesh axis runs over, the one named last changes fastest.
Arguments:
- tokens: bfloat16 [2048, 5120], P('ep', 'grp'), may hold values from -6 to 6
- cotangent: bfloat16 [2048, 5120], P('ep', 'grp'), may hold values from -0.59765625 to 0.59765625
- gate_weights: bfloat16 [2048, 6], P('ep'), may hold values from 0.099609375 to 1
- expert_ids: int32 [2048, 6], P('ep'), may hold values from 0 to 159, all different within a row; in each aligned block of 256 rows (0 to 255, 256 to 511, ...) at most 16 rows name the same one
- hot_ids: int32 [2], replicated, may hold values from 8 to 159, as said below
- gate_cold: bfloat16 [8, 5120, 768], P('ep', 'grp'), may hold values from -0.078125 to 0.078125
- up_cold: bfloat16 [8, 5120, 768], P('ep', 'grp'), may hold values from -0.078125 to 0.078125
- down_cold: bfloat16 [8, 768, 5120], P('ep', None, 'grp'), may hold values from -0.21875 to 0.21875
- gate_hot: bfloat16 [2, 5120, 768], P(None, 'grp', 'ep'), may hold values from -0.078125 to 0.078125
- up_hot: bfloat16 [2, 5120, 768], P(None, 'grp', 'ep'), may hold values from -0.078125 to 0.078125
- down_hot: bfloat16 [2, 768, 5120], P(None, 'ep', 'grp'), may hold values from -0.21875 to 0.21875
Outputs:
- grad_gate_cold: bfloat16 [8, 5120, 768], P('ep', 'grp')
- grad_up_cold: bfloat16 [8, 5120, 768], P('ep', 'grp')
- grad_down_cold: bfloat16 [8, 768, 5120], P('ep', None, 'grp')
- grad_gate_hot: float32 [2, 5120, 768], P(None, 'grp', 'ep')
- grad_up_hot: float32 [2, 5120, 768], P(None, 'grp', 'ep')
- grad_down_hot: float32 [2, 768, 5120], P(None, 'ep', 'grp')
- gate_weight_grad: float32 [2048, 6], P('ep')
Inputs may be any that keep to these rules, and one draw needn't show every extreme that they name: `expert_ids`: each row names 6 different experts. Among the routes of the 256 tokens of one index of ep (aligned blocks of rows) no expert is named more than 16 times, a bound that some block reaches. `hot_ids`: distinct expert numbers, none below 8; expert 160 - 1 is always among them.
All inputs are finite; a program needn't handle non-finite values.
Results may differ from a plain program's by a relative error of at most 0.02.
Values may be sent and summed in bfloat16 or wider, within the bound.
No kernel may reach another device: no remote copies, remote signals or barrier semaphores. Data moves between devices by JAX's collectives and lax.ppermute only.
A program may use at most 128 MiB of HBM per device.

v0:
```python
import jax
import jax.numpy as jnp
from jax import lax
from jax.sharding import PartitionSpec as P


def route_table(flat_ids, targets, capacity):
    matches = (flat_ids[:, None] == targets[None, :]).astype(jnp.int32)
    rank_of = jnp.cumsum(matches, axis=0) - 1
    slot_of = jnp.sum(matches * rank_of, axis=1)
    owner_of = jnp.sum(matches * jnp.arange(targets.shape[0], dtype=jnp.int32)[None, :], axis=1)
    usable = jnp.sum(matches, axis=1) > 0
    row_of = owner_of * capacity + slot_of
    rows_total = targets.shape[0] * capacity
    route_map = (row_of[None, :] == jnp.arange(rows_total, dtype=jnp.int32)[:, None]) & usable[
        None, :
    ]
    return route_map.astype(jnp.float32)


def gather_rows(route_map, tokens, cotangent, flat_weights, tok_rows, top_count):
    per_token = jnp.sum(route_map.reshape(route_map.shape[0], tok_rows, top_count), axis=2)
    token_map = per_token.astype(jnp.bfloat16)
    feat_rows = jnp.dot(token_map, tokens, preferred_element_type=jnp.float32).astype(jnp.bfloat16)
    cotan_rows = jnp.dot(token_map, cotangent, preferred_element_type=jnp.float32).astype(
        jnp.bfloat16
    )
    scale_rows = jnp.dot(
        route_map, flat_weights.astype(jnp.float32), precision=lax.Precision.HIGHEST
    )
    return (feat_rows, cotan_rows, scale_rows.astype(jnp.bfloat16))


def swiglu_back(pre_gate, pre_up, grad_hidden):
    sigmoid_gate = jax.nn.sigmoid(pre_gate)
    activated = pre_gate * sigmoid_gate
    hidden = (activated * pre_up).astype(jnp.bfloat16)
    back_gate = (
        grad_hidden * pre_up * sigmoid_gate * (1.0 + pre_gate * (1.0 - sigmoid_gate))
    ).astype(jnp.bfloat16)
    back_up = (grad_hidden * activated).astype(jnp.bfloat16)
    return (hidden, back_gate, back_up)


def body(
    tokens,
    cotangent,
    gate_weights,
    expert_ids,
    hot_ids,
    gate_cold,
    up_cold,
    down_cold,
    gate_hot,
    up_hot,
    down_hot,
):
    tok_rows, slice_width = tokens.shape
    top_count = expert_ids.shape[1]
    cold_count = lax.axis_size("ep")
    hot_count = hot_ids.shape[0]
    capacity = tok_rows // 16
    flat_ids = expert_ids.reshape(-1)
    flat_weights = gate_weights.reshape(-1)
    cold_map = route_table(flat_ids, jnp.arange(cold_count, dtype=jnp.int32), capacity)
    hot_map = route_table(flat_ids, hot_ids, capacity)
    cold_feats, cold_cotan, cold_scale = gather_rows(
        cold_map, tokens, cotangent, flat_weights, tok_rows, top_count
    )
    hot_feats, hot_cotan, hot_scale = gather_rows(
        hot_map, tokens, cotangent, flat_weights, tok_rows, top_count
    )
    outgoing = (
        cold_feats.reshape(cold_count, capacity, slice_width),
        cold_cotan.reshape(cold_count, capacity, slice_width),
        cold_scale.reshape(cold_count, capacity),
    )
    recv_feats, recv_cotan, recv_scale = (
        lax.all_to_all(outgoing[0], "ep", split_axis=0, concat_axis=0, tiled=True),
        lax.all_to_all(outgoing[1], "ep", split_axis=0, concat_axis=0, tiled=True),
        lax.all_to_all(outgoing[2], "ep", split_axis=0, concat_axis=0, tiled=True),
    )
    recv_feats = recv_feats.reshape(-1, slice_width)
    recv_cotan = recv_cotan.reshape(-1, slice_width)
    weighted = (
        recv_scale.reshape(-1).astype(jnp.float32)[:, None] * recv_cotan.astype(jnp.float32)
    ).astype(jnp.bfloat16)
    w_gate = gate_cold[0]
    w_up = up_cold[0]
    w_down = down_cold[0]
    part_gate = jnp.dot(recv_feats, w_gate, preferred_element_type=jnp.float32)
    part_up = jnp.dot(recv_feats, w_up, preferred_element_type=jnp.float32)
    part_hidden = lax.dot_general(
        weighted, w_down, (((1,), (1,)), ((), ())), preferred_element_type=jnp.float32
    )
    pre_gate, pre_up, grad_hidden = (
        lax.psum(part_gate.astype(jnp.bfloat16), "grp").astype(jnp.float32),
        lax.psum(part_up.astype(jnp.bfloat16), "grp").astype(jnp.float32),
        lax.psum(part_hidden.astype(jnp.bfloat16), "grp").astype(jnp.float32),
    )
    hidden, back_gate, back_up = swiglu_back(pre_gate, pre_up, grad_hidden)
    output_slice = jnp.dot(hidden, w_down, preferred_element_type=jnp.float32)
    cold_route = jnp.sum(output_slice * recv_cotan.astype(jnp.float32), axis=1)
    contract_rows = (((0,), (0,)), ((), ()))
    grad_gate_cold = lax.dot_general(
        recv_feats, back_gate, contract_rows, preferred_element_type=jnp.float32
    )
    grad_up_cold = lax.dot_general(
        recv_feats, back_up, contract_rows, preferred_element_type=jnp.float32
    )
    grad_down_cold = lax.dot_general(
        hidden, weighted, contract_rows, preferred_element_type=jnp.float32
    )
    hot_weighted_local = (
        hot_scale.astype(jnp.float32)[:, None] * hot_cotan.astype(jnp.float32)
    ).astype(jnp.bfloat16)
    blocks = lax.axis_size("ep")
    stacked = jnp.stack([hot_feats, hot_cotan, hot_weighted_local])
    all_rows = lax.all_gather(stacked, "ep", axis=1, tiled=False)
    all_rows = all_rows.reshape(3, blocks, hot_count, capacity, slice_width)
    all_rows = jnp.transpose(all_rows, (0, 2, 1, 3, 4)).reshape(
        3, hot_count, blocks * capacity, slice_width
    )
    rows_feat, rows_cot, rows_wt = (all_rows[0], all_rows[1], all_rows[2])
    part_gate_hot = jnp.einsum(
        "jrd,jdh->jrh", rows_feat, gate_hot, preferred_element_type=jnp.float32
    )
    part_up_hot = jnp.einsum("jrd,jdh->jrh", rows_feat, up_hot, preferred_element_type=jnp.float32)
    part_hidden_hot = jnp.einsum(
        "jrd,jhd->jrh", rows_wt, down_hot, preferred_element_type=jnp.float32
    )
    cot_down = jnp.einsum("jrd,jhd->jrh", rows_cot, down_hot, preferred_element_type=jnp.float32)
    hot_parts = lax.psum(
        jnp.stack([part_gate_hot, part_up_hot, part_hidden_hot]).astype(jnp.bfloat16), "grp"
    ).astype(jnp.float32)
    hidden_hot, back_gate_hot, back_up_hot = swiglu_back(hot_parts[0], hot_parts[1], hot_parts[2])
    hot_route_part = jnp.sum(hidden_hot.astype(jnp.float32) * cot_down, axis=2)
    hidden_blk = hidden_hot.shape[2]
    feat_b = rows_feat.reshape(hot_count, blocks, capacity, slice_width)
    wt_b = rows_wt.reshape(hot_count, blocks, capacity, slice_width)
    bg_b = back_gate_hot.reshape(hot_count, blocks, capacity, hidden_blk)
    bu_b = back_up_hot.reshape(hot_count, blocks, capacity, hidden_blk)
    hid_b = hidden_hot.reshape(hot_count, blocks, capacity, hidden_blk)
    blk_gate = jnp.einsum("jbcd,jbch->jbdh", feat_b, bg_b, preferred_element_type=jnp.float32)
    blk_up = jnp.einsum("jbcd,jbch->jbdh", feat_b, bu_b, preferred_element_type=jnp.float32)
    blk_down = jnp.einsum("jbch,jbcd->jbhd", hid_b, wt_b, preferred_element_type=jnp.float32)
    grad_gate_hot = jnp.sum(blk_gate.astype(jnp.bfloat16).astype(jnp.float32), axis=1)
    grad_up_hot = jnp.sum(blk_up.astype(jnp.bfloat16).astype(jnp.float32), axis=1)
    grad_down_hot = jnp.sum(blk_down.astype(jnp.bfloat16).astype(jnp.float32), axis=1)
    hot_route_all = lax.psum(hot_route_part, ("grp", "ep"))
    me = lax.axis_index("ep")
    hot_route = lax.dynamic_index_in_dim(
        hot_route_all.reshape(hot_count, blocks, capacity), me, axis=1, keepdims=False
    )
    cold_route = lax.psum(cold_route, "grp")
    cold_back = lax.all_to_all(
        cold_route.reshape(cold_count, capacity), "ep", split_axis=0, concat_axis=0, tiled=True
    )
    route_flat = jnp.dot(cold_back.reshape(-1), cold_map, precision=lax.Precision.HIGHEST)
    route_flat = route_flat + jnp.dot(
        hot_route.reshape(-1), hot_map, precision=lax.Precision.HIGHEST
    )
    gate_weight_grad = route_flat.reshape(tok_rows, top_count)
    return (
        grad_gate_cold[None].astype(jnp.bfloat16),
        grad_up_cold[None].astype(jnp.bfloat16),
        grad_down_cold[None].astype(jnp.bfloat16),
        grad_gate_hot,
        grad_up_hot,
        grad_down_hot,
        gate_weight_grad,
    )


def solution(mesh):
    in_specs = (
        P("ep", "grp"),
        P("ep", "grp"),
        P("ep", None),
        P("ep", None),
        P(),
        P("ep", "grp", None),
        P("ep", "grp", None),
        P("ep", None, "grp"),
        P(None, "grp", "ep"),
        P(None, "grp", "ep"),
        P(None, "ep", "grp"),
    )
    out_specs = (
        P("ep", "grp", None),
        P("ep", "grp", None),
        P("ep", None, "grp"),
        P(None, "grp", "ep"),
        P(None, "grp", "ep"),
        P(None, "ep", "grp"),
        P("ep", None),
    )
    return jax.shard_map(body, mesh=mesh, in_specs=in_specs, out_specs=out_specs, check_vma=False)
```

profile of v0, /device:TPU:0, one launch (start us, length us, event | category | flops | bytes accessed | tf_op | source)
XLA Modules:
  0.0 194.5 jit_solution(9976301442183095189)
XLA Ops:
  12.8 1.3 convolution_convert_fusion.8
  15.2 2.3 %reduce-window.14 = s32[8,12,128]{2,1,0:T(8,128)S(1)} reduce-window(s32[8,12,128]{2,1,0:T(8,128)S(1)} %fusion.69, s32[]{:T(128)} %constant.15.clone.1), window={size=1x1x128 pad=0_0x0_0x127_0}, to_apply=%region_1.2 | reduce-window | flops 1560576 | bytes 98308 | tf_op jit(solution)/shard_map/reduce-window
  19.1 7.3 %all-to-all-start.1 = ((bf16[8,1,16]{2,1,0:T(2,128)(2,1)}), bf16[8,1,16]{2,1,0:T(2,128)(2,1)S(1)}, u32[]{:S(2)}, u32[]{:S(2)}) async-start(bf16[8,1,16]{2,1,0:T(2,128)(2,1)} %all_to_all.24), calls=%async_computation.1 | async-start | bytes 8192 | tf_op jit(solution)/shard_map/all_to_all | solution.py:81
  28.0 4.8 %all-to-all-done.1 = bf16[8,1,16]{2,1,0:T(2,128)(2,1)S(1)} async-done(((bf16[8,1,16]{2,1,0:T(2,128)(2,1)}), bf16[8,1,16]{2,1,0:T(2,128)(2,1)S(1)}, u32[]{:S(2)}, u32[]{:S(2)}) %all-to-all-start.1) | async-done | bytes 288 | tf_op jit(solution)/shard_map/all_to_all | solution.py:81
  32.8 3.4 %all-to-all-start = ((bf16[8,16,1280]{2,1,0:T(8,128)(2,1)}), bf16[8,16,1280]{2,1,0:T(8,128)(2,1)S(1)}, u32[]{:S(2)}, u32[]{:S(2)}) async-start(bf16[8,16,1280]{2,1,0:T(8,128)(2,1)} %bitcast.165), calls=%async_computation | async-start | bytes 655360 | tf_op jit(solution)/shard_map/all_to_all | solution.py:79
  37.3 9.1 %all-to-all-done = bf16[8,16,1280]{2,1,0:T(8,128)(2,1)S(1)} async-done(((bf16[8,16,1280]{2,1,0:T(8,128)(2,1)}), bf16[8,16,1280]{2,1,0:T(8,128)(2,1)S(1)}, u32[]{:S(2)}, u32[]{:S(2)}) %all-to-all-start) | async-done | bytes 327712 | tf_op jit(solution)/shard_map/all_to_all | solution.py:79
  46.4 3.9 %all-to-all-start.2 = ((bf16[8,16,1280]{2,1,0:T(8,128)(2,1)}), bf16[8,16,1280]{2,1,0:T(8,128)(2,1)S(1)}, u32[]{:S(2)}, u32[]{:S(2)}) async-start(bf16[8,16,1280]{2,1,0:T(8,128)(2,1)} %bitcast.166), calls=%async_computation.2 | async-start | bytes 655360 | tf_op jit(solution)/shard_map/all_to_all | solution.py:80
  50.3 2.8 %fusion.20 = bf16[128,768]{1,0:T(8,128)(2,1)} fusion(bf16[128,1280]{1,0:T(8,128)(2,1)S(1)} %bitcast.155, bf16[1,1280,768]{2,1,0:T(8,128)(2,1)} %param.16), kind=kOutput, calls=%fused_computation.29 | convolution fusion | flops 251756544 | bytes 2490368 | tf_op jit(solution)/shard_map/dot_general | solution.py:91
  54.3 14.6 %all-to-all-done.2 = bf16[8,16,1280]{2,1,0:T(8,128)(2,1)S(1)} async-done(((bf16[8,16,1280]{2,1,0:T(8,128)(2,1)}), bf16[8,16,1280]{2,1,0:T(8,128)(2,1)S(1)}, u32[]{:S(2)}, u32[]{:S(2)}) %all-to-all-start.2) | async-done | bytes 327712 | tf_op jit(solution)/shard_map/all_to_all | solution.py:80
  69.0 1.5 fusion.14
  70.5 2.1 %all-gather.3.cloned.1.call-done = bf16[3,256,1280]{2,1,0:T(8,128)(2,1)} async-done(((bf16[3,32,1280]{2,1,0:T(8,128)(2,1)}), bf16[3,256,1280]{2,1,0:T(8,128)(2,1)}) %all-gather.3.cloned.1.call-update) | async-done | bytes 1966096 | tf_op jit(solution)/shard_map/all_gather | solution.py:119
  72.6 1.7 copy.68
  78.1 33.6 %all-reduce.3.cloned.1.call-done = (bf16[128,768]{1,0:T(8,128)(2,1)}, bf16[128,768]{1,0:T(8,128)(2,1)}, bf16[128,768]{1,0:T(8,128)(2,1)}, bf16[3,2,128,96]{2,3,1,0:T(8,128)(2,1)}) async-done(((bf16[128,768]{1,0:T(8,128)(2,1)}, bf16[128,768]{1,0:T(8,128)(2,1)}, bf16[128,768]{1,0:T(8,128)(2,1)}, bf16[3,2,128,96]{2,3,1,0:T(8,128)(2,1)}), (bf16[128,768]{1,0:T(8,128)(2,1)}, bf16[128,768]{1,0:T(8,128)(2,1)}, ...) | async-done | bytes 737296 | tf_op jit(solution)/shard_map/psum | solution.py:98
  111.7 1.6 convert_element_type.217
  114.5 3.3 %convert_reduce_fusion = f32[2,96,1280]{2,1,0:T(8,128)} fusion(f32[2,8,16,96]{3,2,1,0:T(8,128)S(1)} %bitcast.169, f32[2,8,16,96]{3,2,1,0:T(8,128)S(1)} %bitcast.171, bf16[3,2,8,16,1280]{4,3,2,1,0:T(8,128)(2,1)} %bitcast.152), kind=kOutput, calls=%fused_computation | convolution fusion | flops 68714496 | bytes 1835008 | tf_op jit(solution)/shard_map/jbch,jbcd->jbhd/dot_general | solution.py:146
  117.8 3.3 %convert_reduce_fusion.2 = f32[2,1280,96]{1,2,0:T(8,128)} fusion(f32[2,8,16,96]{3,2,1,0:T(8,128)S(1)} %bitcast.172, f32[2,8,16,96]{3,2,1,0:T(8,128)S(1)} %bitcast.174, f32[2,8,16,96]{3,2,1,0:T(8,128)S(1)} %bitcast.170, bf16[3,2,8,16,1280]{4,3,2,1,0:T(8,128)(2,1)} %bitcast.153), kind=kOutput, calls=%fused_computation.2 | convolution fusion | flops 68812800 | bytes 1933312 | tf_op jit(solution)/shard_map/jbcd,jbch->jbdh/dot_general | solution.py:144
  121.1 3.4 %convert_reduce_fusion.1 = f32[2,1280,96]{1,2,0:T(8,128)} fusion(f32[2,8,16,96]{3,2,1,0:T(8,128)S(1)} %bitcast.175, f32[2,8,16,96]{3,2,1,0:T(8,128)S(1)} %bitcast.173, bf16[3,2,8,16,1280]{4,3,2,1,0:T(8,128)(2,1)} %bitcast.154), kind=kOutput, calls=%fused_computation.1 | convolution fusion | flops 68714496 | bytes 1835008 | tf_op jit(solution)/shard_map/jbcd,jbch->jbdh/dot_general | solution.py:145
  124.6 2.0 %fusion.1 = bf16[1,1280,768]{2,1,0:T(8,128)(2,1)} fusion(bf16[128,1280]{1,0:T(8,128)(2,1)S(1)} %bitcast.157, bf16[128,768]{1,0:T(8,128)(2,1)S(1)} %copy-done.7, bf16[128,768]{1,0:T(8,128)(2,1)S(1)} %copy-done.5), kind=kOutput, calls=%fused_computation.10 | convolution fusion | flops 253427712 | bytes 2686976 | tf_op jit(solution)/shard_map/dot_general | solution.py:108
  126.5 2.0 %fusion = bf16[1,1280,768]{2,1,0:T(8,128)(2,1)} fusion(bf16[128,1280]{1,0:T(8,128)(2,1)S(1)} %bitcast.158, bf16[128,768]{1,0:T(8,128)(2,1)S(1)} %copy-done.6, bf16[128,768]{1,0:T(8,128)(2,1)S(1)} %copy-done.7, bf16[128,768]{1,0:T(8,128)(2,1)S(1)} %copy-done.5), kind=kOutput, calls=%fused_computation.9 | convolution fusion | flops 253919232 | bytes 2883584 | tf_op jit(solution)/shard_map/dot_general | solution.py:105
  129.2 6.2 %psum.46 = f32[8,1,16]{2,0,1:T(8,128)} all-reduce(f32[8,1,16]{2,0,1:T(8,128)S(1)} %all_to_all.22), channel_id=1, replica_groups=mesh['grp'=4,'ep'=8] {'grp'}, use_global_device_ids=true, to_apply=%region_20.21 | all-reduce | flops 128 | bytes 1024 | tf_op jit(solution)/shard_map/psum | solution.py:155
  135.4 5.5 %all-to-all-start.3 = ((f32[8,1,16]{2,1,0:T(1,128)}), f32[8,1,16]{2,1,0:T(1,128)S(1)}, u32[]{:S(2)}, u32[]{:S(2)}) async-start(f32[8,1,16]{2,1,0:T(1,128)} %bitcast.31), calls=%async_computation.3 | async-start | bytes 8192 | tf_op jit(solution)/shard_map/all_to_all | solution.py:156
  140.9 1.6 fusion.23
  142.6 40.2 %psum.47 = f32[2,8,16]{2,1,0:T(8,128)S(1)} all-reduce(f32[2,8,16]{2,1,0:T(8,128)S(1)} %reshape.204), channel_id=1, replica_groups=mesh['grp'=4,'ep'=8] {'grp','ep'}, use_global_device_ids=true, to_apply=%region_22.23 | all-reduce | flops 256 | bytes 2048 | tf_op jit(solution)/shard_map/psum | solution.py:150
  183.0 2.0 %fusion.2 = bf16[1,768,1280]{2,1,0:T(8,128)(2,1)} fusion(bf16[128,1280]{1,0:T(8,128)(2,1)S(1)} %fusion.37, bf16[128,768]{1,0:T(8,128)(2,1)S(1)} %copy-done.6, bf16[128,768]{1,0:T(8,128)(2,1)S(1)} %copy-done.5), kind=kOutput, calls=%fused_computation.11 | convolution fusion | flops 253427712 | bytes 2686976 | tf_op jit(solution)/shard_map/dot_general | solution.py:111
  (92 shorter events, 20.4 us)
Async XLA Ops:
  7.2 61.9 %copy-start = (bf16[1,768,1280]{2,1,0:T(8,128)(2,1)S(1)}, bf16[1,768,1280]{2,1,0:T(8,128)(2,1)}, u32[]{:S(2)}) copy-start(bf16[1,768,1280]{2,1,0:T(8,128)(2,1)} %param.18) | copy-start | bytes 5898244
  7.2 6.9 %copy-start.2 = (bf16[256,1280]{1,0:T(8,128)(2,1)S(1)}, bf16[256,1280]{1,0:T(8,128)(2,1)}, u32[]{:S(2)}) copy-start(bf16[256,1280]{1,0:T(8,128)(2,1)} %param.11) | copy-start | bytes 1966084
  7.2 65.4 %all-gather.3.cloned.1.call-start = ((), (), s32[]{:S(2)}) async-start(), calls=%async_computation.4 | async-start | bytes 2211840 | tf_op jit(solution)/shard_map/all_gather | solution.py:119
  14.4 21.8 %copy-start.3 = (bf16[256,1280]{1,0:T(8,128)(2,1)S(1)}, bf16[256,1280]{1,0:T(8,128)(2,1)}, u32[]{:S(2)}) copy-start(bf16[256,1280]{1,0:T(8,128)(2,1)} %param.12) | copy-start | bytes 1966084
  19.1 13.7 %all-to-all-start.1 = ((bf16[8,1,16]{2,1,0:T(2,128)(2,1)}), bf16[8,1,16]{2,1,0:T(2,128)(2,1)S(1)}, u32[]{:S(2)}, u32[]{:S(2)}) async-start(bf16[8,1,16]{2,1,0:T(2,128)(2,1)} %all_to_all.24), calls=%async_computation.1 | async-start | bytes 8192 | tf_op jit(solution)/shard_map/all_to_all | solution.py:81
  32.8 13.6 %all-to-all-start = ((bf16[8,16,1280]{2,1,0:T(8,128)(2,1)}), bf16[8,16,1280]{2,1,0:T(8,128)(2,1)S(1)}, u32[]{:S(2)}, u32[]{:S(2)}) async-start(bf16[8,16,1280]{2,1,0:T(8,128)(2,1)} %bitcast.165), calls=%async_computation | async-start | bytes 655360 | tf_op jit(solution)/shard_map/all_to_all | solution.py:79
  46.4 22.5 %all-to-all-start.2 = ((bf16[8,16,1280]{2,1,0:T(8,128)(2,1)}), bf16[8,16,1280]{2,1,0:T(8,128)(2,1)S(1)}, u32[]{:S(2)}, u32[]{:S(2)}) async-start(bf16[8,16,1280]{2,1,0:T(8,128)(2,1)} %bitcast.166), calls=%async_computation.2 | async-start | bytes 655360 | tf_op jit(solution)/shard_map/all_to_all | solution.py:80
  50.3 61.4 %all-reduce.3.cloned.1.call-start = ((), (), s32[]{:S(2)}) async-start(), calls=%async_computation.5 | async-start | bytes 1474560 | tf_op jit(solution)/shard_map/psum | solution.py:98
  50.3 2.8 %copy-start.4 = (bf16[1,1280,768]{2,1,0:T(8,128)(2,1)S(1)}, bf16[1,1280,768]{2,1,0:T(8,128)(2,1)}, u32[]{:S(2)}) copy-start(bf16[1,1280,768]{2,1,0:T(8,128)(2,1)} %param.17) | copy-start | bytes 5898244
  74.3 1.5 copy-start.1
  74.3 1.5 copy-start.8
  74.4 1.9 copy-start.9
  75.8 1.1 copy-start.10
  121.1 3.4 %copy-start.5 = (bf16[128,768]{1,0:T(8,128)(2,1)S(1)}, bf16[128,768]{1,0:T(8,128)(2,1)}, u32[]{:S(2)}) copy-start(bf16[128,768]{1,0:T(8,128)(2,1)} %get-tuple-element.36) | copy-start | bytes 589828
  121.1 3.4 %copy-start.7 = (bf16[128,768]{1,0:T(8,128)(2,1)S(1)}, bf16[128,768]{1,0:T(8,128)(2,1)}, u32[]{:S(2)}) copy-start(bf16[128,768]{1,0:T(8,128)(2,1)} %get-tuple-element.35) | copy-start | bytes 589828
  124.5 2.0 %copy-start.6 = (bf16[128,768]{1,0:T(8,128)(2,1)S(1)}, bf16[128,768]{1,0:T(8,128)(2,1)}, u32[]{:S(2)}) copy-start(bf16[128,768]{1,0:T(8,128)(2,1)} %get-tuple-element.34) | copy-start | bytes 589828
  135.4 49.7 %all-to-all-start.3 = ((f32[8,1,16]{2,1,0:T(1,128)}), f32[8,1,16]{2,1,0:T(1,128)S(1)}, u32[]{:S(2)}, u32[]{:S(2)}) async-start(f32[8,1,16]{2,1,0:T(1,128)} %bitcast.31), calls=%async_computation.3 | async-start | bytes 8192 | tf_op jit(solution)/shard_map/all_to_all | solution.py:156
Sparse Core Ops, SparseCore 0:
  15.3 57.2 all-gather.2
  78.1 33.5 all-reduce.2
where the time goes:
time: 195 us
  waiting for transfers between devices  64.2 us (33%)
  blocking collectives  46.4 us (24%)
  matrix products  29.2 us (15%)
  starting transfers between devices  20.2 us (10%)
  between operations  14.4 us (7%)
  local copies, waits for them, and re-layouts  10.9 us (6%)
  other arithmetic  9.22 us (5%)
    psum x1, blocking collectives, body(): hot_route_all = lax.psum(hot_route_part, ('grp', 'ep'))  40.2 us
    psum x1, waiting for transfers between devices, body(): lax.psum(part_up.astype(jnp.bfloat16), 'grp').astype(jnp.float32)  33.6 us
    all_to_all x1, waiting for transfers between devices, body(): lax.all_to_all(outgoing[1], 'ep', split_axis=0, concat_axis=0, tiled=True)  14.6 us
    all_to_all x1, waiting for transfers between devices, body(): lax.all_to_all(outgoing[0], 'ep', split_axis=0, concat_axis=0, tiled=True)  9.11 us
    all_to_all x1, starting transfers between devices, body(): lax.all_to_all(outgoing[2], 'ep', split_axis=0, concat_axis=0, tiled=True)  7.28 us
    psum x1, blocking collectives, body(): cold_route = lax.psum(cold_route, 'grp')  6.24 us
    all_to_all x1, starting transfers between devices, body(): lax.all_to_all(cold_route.reshape(cold_count, capacity), 'ep', split_axis...  5.52 us
    all_to_all x1, waiting for transfers between devices, body(): lax.all_to_all(outgoing[2], 'ep', split_axis=0, concat_axis=0, tiled=True)  4.77 us
  transfers between devices with their start and end apart: 6, of which 5 were waited for; matrix products, arithmetic and copies ran while one was open for 8% of the time, Pallas kernels for 0%

commit v1 on v0

--- a/solution.py
+++ b/solution.py
@@ -147,7 +147,7 @@
     grad_gate_hot = jnp.sum(blk_gate.astype(jnp.bfloat16).astype(jnp.float32), axis=1)
     grad_up_hot = jnp.sum(blk_up.astype(jnp.bfloat16).astype(jnp.float32), axis=1)
     grad_down_hot = jnp.sum(blk_down.astype(jnp.bfloat16).astype(jnp.float32), axis=1)
-    hot_route_all = lax.psum(hot_route_part, ("grp", "ep"))
+    hot_route_all = lax.psum(lax.psum(hot_route_part, "ep"), "grp")
     me = lax.axis_index("ep")
     hot_route = lax.dynamic_index_in_dim(
         hot_route_all.reshape(hot_count, blocks, capacity), me, axis=1, keepdims=False

time: 195 us -> 183 us (0.938)
  blocking collectives: 46.4 us -> 32.1 us
  waiting for transfers between devices: 64.2 us -> 68.3 us
  starting transfers between devices: 20.2 us -> 18 us
    psum x1, blocking collectives: 40.2 us -> 21.4 us  [body(): hot_route_all = lax.psum(lax.psum(hot_route_part, 'ep'), 'grp')]
    psum x1, blocking collectives: 6.24 us -> 10.7 us  [body(): cold_route = lax.psum(cold_route, 'grp')]
    all_to_all x1, waiting for transfers between devices: 0.01 us -> 4.11 us  [body(): lax.all_to_all(cold_route.reshape(cold_count, capacity), 'ep', split_axis...]
    all_to_all x1, starting transfers between devices: 5.52 us -> 3.31 us  [body(): lax.all_to_all(cold_route.reshape(cold_count, capacity), 'ep', split_axis...]
  transfers between devices with their start and end apart: 6 -> 6, of which waited for: 5 -> 6; matrix products, arithmetic and copies ran while one was open for 8% -> 8% of each run, Pallas kernels for 0% -> 0%
where the time goes in v1:
time: 183 us; the launch traced here: 182 us
  waiting for transfers between devices  68.3 us (37%)
  blocking collectives  32.1 us (18%)
  matrix products  29.2 us (16%)
  starting transfers between devices  18 us (10%)
  between operations  14.4 us (8%)
  local copies, waits for them, and re-layouts  10.9 us (6%)
  other arithmetic  9.22 us (5%)
    psum x1, waiting for transfers between devices, body(): lax.psum(part_up.astype(jnp.bfloat16), 'grp').astype(jnp.float32)  33.6 us
    psum x1, blocking collectives, body(): hot_route_all = lax.psum(lax.psum(hot_route_part, 'ep'), 'grp')  21.4 us
    all_to_all x1, waiting for transfers between devices, body(): lax.all_to_all(outgoing[1], 'ep', split_axis=0, concat_axis=0, tiled=True)  14.6 us
    psum x1, blocking collectives, body(): cold_route = lax.psum(cold_route, 'grp')  10.7 us
    all_to_all x1, waiting for transfers between devices, body(): lax.all_to_all(outgoing[0], 'ep', split_axis=0, concat_axis=0, tiled=True)  9.11 us
    all_to_all x1, starting transfers between devices, body(): lax.all_to_all(outgoing[2], 'ep', split_axis=0, concat_axis=0, tiled=True)  7.28 us
    all_to_all x1, waiting for transfers between devices, body(): lax.all_to_all(outgoing[2], 'ep', split_axis=0, concat_axis=0, tiled=True)  4.77 us
    all_to_all x1, waiting for transfers between devices, body(): lax.all_to_all(cold_route.reshape(cold_count, capacity), 'ep', split_axis...  4.11 us
  transfers between devices with their start and end apart: 6, of which 6 were waited for; matrix products, arithmetic and copies ran while one was open for 8% of the time, Pallas kernels for 0%

profile of v1, /device:TPU:0, one launch (start us, length us, event | category | flops | bytes accessed | tf_op | source)
XLA Modules:
  0.0 182.1 jit_solution(12595181950888592070)
XLA Ops:
  15.2 2.3 %reduce-window.14 = s32[8,12,128]{2,1,0:T(8,128)S(1)} reduce-window(s32[8,12,128]{2,1,0:T(8,128)S(1)} %fusion.69, s32[]{:T(128)} %constant.15.clone.1), window={size=1x1x128 pad=0_0x0_0x127_0}, to_apply=%region_1.2 | reduce-window | flops 1560576 | bytes 98308 | tf_op jit(solution)/shard_map/reduce-window
  19.1 7.3 %all-to-all-start.1 = ((bf16[8,1,16]{2,1,0:T(2,128)(2,1)}), bf16[8,1,16]{2,1,0:T(2,128)(2,1)S(1)}, u32[]{:S(2)}, u32[]{:S(2)}) async-start(bf16[8,1,16]{2,1,0:T(2,128)(2,1)} %all_to_all.24), calls=%async_computation.1 | async-start | bytes 8192 | tf_op jit(solution)/shard_map/all_to_all | solution.py:81
  28.0 4.8 %all-to-all-done.1 = bf16[8,1,16]{2,1,0:T(2,128)(2,1)S(1)} async-done(((bf16[8,1,16]{2,1,0:T(2,128)(2,1)}), bf16[8,1,16]{2,1,0:T(2,128)(2,1)S(1)}, u32[]{:S(2)}, u32[]{:S(2)}) %all-to-all-start.1) | async-done | bytes 288 | tf_op jit(solution)/shard_map/all_to_all | solution.py:81
  32.8 3.4 %all-to-all-start = ((bf16[8,16,1280]{2,1,0:T(8,128)(2,1)}), bf16[8,16,1280]{2,1,0:T(8,128)(2,1)S(1)}, u32[]{:S(2)}, u32[]{:S(2)}) async-start(bf16[8,16,1280]{2,1,0:T(8,128)(2,1)} %bitcast.165), calls=%async_computation | async-start | bytes 655360 | tf_op jit(solution)/shard_map/all_to_all | solution.py:79
  37.3 9.1 %all-to-all-done = bf16[8,16,1280]{2,1,0:T(8,128)(2,1)S(1)} async-done(((bf16[8,16,1280]{2,1,0:T(8,128)(2,1)}), bf16[8,16,1280]{2,1,0:T(8,128)(2,1)S(1)}, u32[]{:S(2)}, u32[]{:S(2)}) %all-to-all-start) | async-done | bytes 327712 | tf_op jit(solution)/shard_map/all_to_all | solution.py:79
  46.4 3.9 %all-to-all-start.2 = ((bf16[8,16,1280]{2,1,0:T(8,128)(2,1)}), bf16[8,16,1280]{2,1,0:T(8,128)(2,1)S(1)}, u32[]{:S(2)}, u32[]{:S(2)}) async-start(bf16[8,16,1280]{2,1,0:T(8,128)(2,1)} %bitcast.166), calls=%async_computation.2 | async-start | bytes 655360 | tf_op jit(solution)/shard_map/all_to_all | solution.py:80
  50.3 2.8 %fusion.20 = bf16[128,768]{1,0:T(8,128)(2,1)} fusion(bf16[128,1280]{1,0:T(8,128)(2,1)S(1)} %bitcast.155, bf16[1,1280,768]{2,1,0:T(8,128)(2,1)} %param.16), kind=kOutput, calls=%fused_computation.29 | convolution fusion | flops 251756544 | bytes 2490368 | tf_op jit(solution)/shard_map/dot_general | solution.py:91
  54.3 14.6 %all-to-all-done.2 = bf16[8,16,1280]{2,1,0:T(8,128)(2,1)S(1)} async-done(((bf16[8,16,1280]{2,1,0:T(8,128)(2,1)}), bf16[8,16,1280]{2,1,0:T(8,128)(2,1)S(1)}, u32[]{:S(2)}, u32[]{:S(2)}) %all-to-all-start.2) | async-done | bytes 327712 | tf_op jit(solution)/shard_map/all_to_all | solution.py:80
  69.0 1.5 fusion.14
  70.5 2.1 %all-gather.3.cloned.1.call-done = bf16[3,256,1280]{2,1,0:T(8,128)(2,1)} async-done(((bf16[3,32,1280]{2,1,0:T(8,128)(2,1)}), bf16[3,256,1280]{2,1,0:T(8,128)(2,1)}) %all-gather.3.cloned.1.call-update) | async-done | bytes 1966096 | tf_op jit(solution)/shard_map/all_gather | solution.py:119
  72.6 1.7 copy.68
  78.1 33.6 %all-reduce.4.cloned.1.call-done = (bf16[128,768]{1,0:T(8,128)(2,1)}, bf16[128,768]{1,0:T(8,128)(2,1)}, bf16[128,768]{1,0:T(8,128)(2,1)}, bf16[3,2,128,96]{2,3,1,0:T(8,128)(2,1)}) async-done(((bf16[128,768]{1,0:T(8,128)(2,1)}, bf16[128,768]{1,0:T(8,128)(2,1)}, bf16[128,768]{1,0:T(8,128)(2,1)}, bf16[3,2,128,96]{2,3,1,0:T(8,128)(2,1)}), (bf16[128,768]{1,0:T(8,128)(2,1)}, bf16[128,768]{1,0:T(8,128)(2,1)}, ...) | async-done | bytes 737296 | tf_op jit(solution)/shard_map/psum | solution.py:98
  111.7 1.6 convert_element_type.217
  114.5 3.3 %convert_reduce_fusion = f32[2,96,1280]{2,1,0:T(8,128)} fusion(f32[2,8,16,96]{3,2,1,0:T(8,128)S(1)} %bitcast.169, f32[2,8,16,96]{3,2,1,0:T(8,128)S(1)} %bitcast.171, bf16[3,2,8,16,1280]{4,3,2,1,0:T(8,128)(2,1)} %bitcast.152), kind=kOutput, calls=%fused_computation | convolution fusion | flops 68714496 | bytes 1835008 | tf_op jit(solution)/shard_map/jbch,jbcd->jbhd/dot_general | solution.py:146
  117.8 3.3 %convert_reduce_fusion.2 = f32[2,1280,96]{1,2,0:T(8,128)} fusion(f32[2,8,16,96]{3,2,1,0:T(8,128)S(1)} %bitcast.172, f32[2,8,16,96]{3,2,1,0:T(8,128)S(1)} %bitcast.174, f32[2,8,16,96]{3,2,1,0:T(8,128)S(1)} %bitcast.170, bf16[3,2,8,16,1280]{4,3,2,1,0:T(8,128)(2,1)} %bitcast.153), kind=kOutput, calls=%fused_computation.2 | convolution fusion | flops 68812800 | bytes 1933312 | tf_op jit(solution)/shard_map/jbcd,jbch->jbdh/dot_general | solution.py:144
  121.1 3.4 %convert_reduce_fusion.1 = f32[2,1280,96]{1,2,0:T(8,128)} fusion(f32[2,8,16,96]{3,2,1,0:T(8,128)S(1)} %bitcast.175, f32[2,8,16,96]{3,2,1,0:T(8,128)S(1)} %bitcast.173, bf16[3,2,8,16,1280]{4,3,2,1,0:T(8,128)(2,1)} %bitcast.154), kind=kOutput, calls=%fused_computation.1 | convolution fusion | flops 68714496 | bytes 1835008 | tf_op jit(solution)/shard_map/jbcd,jbch->jbdh/dot_general | solution.py:145
  124.6 2.0 %fusion.1 = bf16[1,1280,768]{2,1,0:T(8,128)(2,1)} fusion(bf16[128,1280]{1,0:T(8,128)(2,1)S(1)} %bitcast.157, bf16[128,768]{1,0:T(8,128)(2,1)S(1)} %copy-done.7, bf16[128,768]{1,0:T(8,128)(2,1)S(1)} %copy-done.5), kind=kOutput, calls=%fused_computation.10 | convolution fusion | flops 253427712 | bytes 2686976 | tf_op jit(solution)/shard_map/dot_general | solution.py:108
  126.5 2.0 %fusion = bf16[1,1280,768]{2,1,0:T(8,128)(2,1)} fusion(bf16[128,1280]{1,0:T(8,128)(2,1)S(1)} %bitcast.158, bf16[128,768]{1,0:T(8,128)(2,1)S(1)} %copy-done.6, bf16[128,768]{1,0:T(8,128)(2,1)S(1)} %copy-done.7, bf16[128,768]{1,0:T(8,128)(2,1)S(1)} %copy-done.5), kind=kOutput, calls=%fused_computation.9 | convolution fusion | flops 253919232 | bytes 2883584 | tf_op jit(solution)/shard_map/dot_general | solution.py:105
  129.2 1.6 fusion.23
  130.8 21.4 %psum.54 = f32[2,128]{1,0:T(2,128)S(1)} all-reduce(f32[2,128]{1,0:T(2,128)S(1)} %fusion.23), channel_id=1, replica_groups=mesh['grp'=4,'ep'=8] {'ep'}, use_global_device_ids=true, to_apply=%region_22.23 | all-reduce | flops 256 | bytes 2048 | tf_op jit(solution)/shard_map/psum | solution.py:150
  152.3 10.7 %all-reduce = (f32[8,1,16]{2,0,1:T(8,128)}, f32[2,8,16]{2,1,0:T(8,128)S(1)}) all-reduce(f32[8,1,16]{2,0,1:T(8,128)S(1)} %all_to_all.22, f32[2,8,16]{2,1,0:T(8,128)S(1)} %reshape.204), channel_id=1, replica_groups=mesh['grp'=4,'ep'=8] {'grp'}, use_global_device_ids=true, to_apply=%region_20.21 | all-reduce | flops 384 | bytes 3072 | tf_op jit(solution)/shard_map/psum | solution.py:155
  163.1 3.3 %all-to-all-start.3 = ((f32[8,1,16]{2,1,0:T(1,128)}), f32[8,1,16]{2,1,0:T(1,128)S(1)}, u32[]{:S(2)}, u32[]{:S(2)}) async-start(f32[8,1,16]{2,1,0:T(1,128)} %bitcast.31), calls=%async_computation.3 | async-start | bytes 8192 | tf_op jit(solution)/shard_map/all_to_all | solution.py:156
  166.4 2.0 %fusion.2 = bf16[1,768,1280]{2,1,0:T(8,128)(2,1)} fusion(bf16[128,1280]{1,0:T(8,128)(2,1)S(1)} %fusion.37, bf16[128,768]{1,0:T(8,128)(2,1)S(1)} %copy-done.6, bf16[128,768]{1,0:T(8,128)(2,1)S(1)} %copy-done.5), kind=kOutput, calls=%fused_computation.11 | convolution fusion | flops 253427712 | bytes 2686976 | tf_op jit(solution)/shard_map/dot_general | solution.py:111
  168.6 4.1 %all-to-all-done.3 = f32[8,1,16]{2,1,0:T(1,128)S(1)} async-done(((f32[8,1,16]{2,1,0:T(1,128)}), f32[8,1,16]{2,1,0:T(1,128)S(1)}, u32[]{:S(2)}, u32[]{:S(2)}) %all-to-all-start.3) | async-done | bytes 544 | tf_op jit(solution)/shard_map/all_to_all | solution.py:156
  (92 shorter events, 21.8 us)
Async XLA Ops:
  7.2 61.9 %copy-start = (bf16[1,768,1280]{2,1,0:T(8,128)(2,1)S(1)}, bf16[1,768,1280]{2,1,0:T(8,128)(2,1)}, u32[]{:S(2)}) copy-start(bf16[1,768,1280]{2,1,0:T(8,128)(2,1)} %param.18) | copy-start | bytes 5898244
  7.2 6.9 %copy-start.2 = (bf16[256,1280]{1,0:T(8,128)(2,1)S(1)}, bf16[256,1280]{1,0:T(8,128)(2,1)}, u32[]{:S(2)}) copy-start(bf16[256,1280]{1,0:T(8,128)(2,1)} %param.11) | copy-start | bytes 1966084
  7.2 65.4 %all-gather.3.cloned.1.call-start = ((), (), s32[]{:S(2)}) async-start(), calls=%async_computation.4 | async-start | bytes 2211840 | tf_op jit(solution)/shard_map/all_gather | solution.py:119
  14.4 21.8 %copy-start.3 = (bf16[256,1280]{1,0:T(8,128)(2,1)S(1)}, bf16[256,1280]{1,0:T(8,128)(2,1)}, u32[]{:S(2)}) copy-start(bf16[256,1280]{1,0:T(8,128)(2,1)} %param.12) | copy-start | bytes 1966084
  19.1 13.7 %all-to-all-start.1 = ((bf16[8,1,16]{2,1,0:T(2,128)(2,1)}), bf16[8,1,16]{2,1,0:T(2,128)(2,1)S(1)}, u32[]{:S(2)}, u32[]{:S(2)}) async-start(bf16[8,1,16]{2,1,0:T(2,128)(2,1)} %all_to_all.24), calls=%async_computation.1 | async-start | bytes 8192 | tf_op jit(solution)/shard_map/all_to_all | solution.py:81
  32.8 13.6 %all-to-all-start = ((bf16[8,16,1280]{2,1,0:T(8,128)(2,1)}), bf16[8,16,1280]{2,1,0:T(8,128)(2,1)S(1)}, u32[]{:S(2)}, u32[]{:S(2)}) async-start(bf16[8,16,1280]{2,1,0:T(8,128)(2,1)} %bitcast.165), calls=%async_computation | async-start | bytes 655360 | tf_op jit(solution)/shard_map/all_to_all | solution.py:79
  46.4 22.5 %all-to-all-start.2 = ((bf16[8,16,1280]{2,1,0:T(8,128)(2,1)}), bf16[8,16,1280]{2,1,0:T(8,128)(2,1)S(1)}, u32[]{:S(2)}, u32[]{:S(2)}) async-start(bf16[8,16,1280]{2,1,0:T(8,128)(2,1)} %bitcast.166), calls=%async_computation.2 | async-start | bytes 655360 | tf_op jit(solution)/shard_map/all_to_all | solution.py:80
  50.3 61.4 %all-reduce.4.cloned.1.call-start = ((), (), s32[]{:S(2)}) async-start(), calls=%async_computation.5 | async-start | bytes 1474560 | tf_op jit(solution)/shard_map/psum | solution.py:98
  50.3 2.8 %copy-start.4 = (bf16[1,1280,768]{2,1,0:T(8,128)(2,1)S(1)}, bf16[1,1280,768]{2,1,0:T(8,128)(2,1)}, u32[]{:S(2)}) copy-start(bf16[1,1280,768]{2,1,0:T(8,128)(2,1)} %param.17) | copy-start | bytes 5898244
  74.3 1.5 copy-start.1
  74.3 1.5 copy-start.8
  74.4 1.9 %copy-start.9 = (bf16[2,1280,96]{1,2,0:T(8,128)(2,1)S(1)}, bf16[2,1280,96]{1,2,0:T(8,128)(2,1)}, u32[]{:S(2)}) copy-start(bf16[2,1280,96]{1,2,0:T(8,128)(2,1)} %param.19) | copy-start | bytes 1474564
  75.8 1.1 copy-start.10
  121.1 3.4 %copy-start.5 = (bf16[128,768]{1,0:T(8,128)(2,1)S(1)}, bf16[128,768]{1,0:T(8,128)(2,1)}, u32[]{:S(2)}) copy-start(bf16[128,768]{1,0:T(8,128)(2,1)} %get-tuple-element.38) | copy-start | bytes 589828
  121.1 3.4 %copy-start.7 = (bf16[128,768]{1,0:T(8,128)(2,1)S(1)}, bf16[128,768]{1,0:T(8,128)(2,1)}, u32[]{:S(2)}) copy-start(bf16[128,768]{1,0:T(8,128)(2,1)} %get-tuple-element.37) | copy-start | bytes 589828
  124.5 2.0 %copy-start.6 = (bf16[128,768]{1,0:T(8,128)(2,1)S(1)}, bf16[128,768]{1,0:T(8,128)(2,1)}, u32[]{:S(2)}) copy-start(bf16[128,768]{1,0:T(8,128)(2,1)} %get-tuple-element.36) | copy-start | bytes 589828
  163.1 9.6 %all-to-all-start.3 = ((f32[8,1,16]{2,1,0:T(1,128)}), f32[8,1,16]{2,1,0:T(1,128)S(1)}, u32[]{:S(2)}, u32[]{:S(2)}) async-start(f32[8,1,16]{2,1,0:T(1,128)} %bitcast.31), calls=%async_computation.3 | async-start | bytes 8192 | tf_op jit(solution)/shard_map/all_to_all | solution.py:156
Sparse Core Ops, SparseCore 0:
  15.3 57.2 all-gather.2
  78.1 33.5 all-reduce.3
